TPU v7x, 128 devices: a whole 4x4x4 slice. The times are simulated.
128 devices in a mesh: space: 32 (over x, z, core), feat: 4 (over y).
Axes of the slice: x: 4, y: 4, z: 4, core: 2. Of those that a mesh axis runs over, the one named last changes fastest.
Arguments:
- inputs: bfloat16 [2, 96, 180, 1024], P(None, 'space', None, 'feat'), may hold values from -15 to 15
- cotangent: bfloat16 [2, 96, 180, 1024], P(None, 'space', None, 'feat'), may hold values from -6 to 6
- spec_w1: float32 [2, 8, 128, 128], P(None, 'feat'), may hold values from -0.375 to 0.375
- spec_b1: float32 [2, 1024], P(None, 'feat'), may hold values from -0.3 to 0.3
- spec_w2: float32 [2, 8, 128, 128], P(None, 'feat'), may hold values from -0.375 to 0.375
- spec_b2: float32 [2, 1024], P(None, 'feat'), may hold values from -0.3 to 0.3
- up_weight: bfloat16 [1024, 4096], P(None, 'feat'), may hold values from -0.1875 to 0.1875
- down_weight: bfloat16 [4096, 1024], P('feat'), may hold values from -0.09375 to 0.09375
Outputs:
- output: bfloat16 [2, 96, 180, 1024], P(None, 'space', None, 'feat')
- grad_input: bfloat16 [2, 96, 180, 1024], P(None, 'space', None, 'feat')
All inputs are finite; a program needn't handle non-finite values.
Results may differ from a plain program's by a relative error of at most 0.0102.
Values may be sent and summed in bfloat16 or wider, within the bound.
No kernel may reach another device: no remote copies, remote signals or barrier semaphores. Data moves between devices by JAX's collectives and lax.ppermute only.
A program may use at most 128 MiB of HBM per device.

v0:
```python
import math
import jax
import jax.numpy as jnp
from jax import lax
from jax.sharding import PartitionSpec as P

EPSILON = 1e-05
SHRINK_LEVEL = 0.1
HIGHEST = lax.Precision.HIGHEST


def longitude_tables(width_lon):
    mode_count = width_lon // 2 + 1
    cell_index = jnp.arange(width_lon, dtype=jnp.int32)[:, None]
    wave_number = jnp.arange(mode_count, dtype=jnp.int32)[None, :]
    phase_angle = (
        2.0 * math.pi / width_lon * (cell_index * wave_number % width_lon).astype(jnp.float32)
    )
    scaling = 1.0 / math.sqrt(width_lon)
    cos_fwd = jnp.cos(phase_angle) * scaling
    sin_fwd = -jnp.sin(phase_angle) * scaling
    doubled = jnp.where((wave_number == 0) | (wave_number * 2 == width_lon), 1.0, 2.0).astype(
        jnp.float32
    )
    return (cos_fwd, sin_fwd, cos_fwd * doubled, sin_fwd * doubled)


def padded_tables(width_lon, multiple):
    tables = longitude_tables(width_lon)
    modes = tables[0].shape[1]
    extra = -modes % multiple
    return tuple((jnp.pad(table, ((0, 0), (0, extra))) for table in tables))


def lat_apply(table, field):
    return jnp.einsum("gh,bhkc->bgkc", table, field, precision=HIGHEST)


def complex_latitude(table_cos, table_sin, real_part, imag_part, inverse):
    if inverse:
        return (
            lat_apply(table_cos, real_part) + lat_apply(table_sin, imag_part),
            lat_apply(table_cos, imag_part) - lat_apply(table_sin, real_part),
        )
    return (
        lat_apply(table_cos, real_part) - lat_apply(table_sin, imag_part),
        lat_apply(table_cos, imag_part) + lat_apply(table_sin, real_part),
    )


def lon_forward(field, table):
    return jnp.einsum("brwc,wk->brkc", field, table, precision=HIGHEST)


def lon_back(spec, table):
    return jnp.einsum("brkc,wk->brwc", spec, table, precision=HIGHEST)


def to_blocks(field, block_size):
    return field.reshape(field.shape[:-1] + (field.shape[-1] // block_size, block_size))


def block_mult(field, weights):
    return jnp.einsum("...nc,nce->...ne", field, weights, precision=HIGHEST)


def block_mult_back(field, weights):
    return jnp.einsum("...ne,nce->...nc", field, weights, precision=HIGHEST)


def block_product(real_part, imag_part, weights):
    return (
        block_mult(real_part, weights[0]) - block_mult(imag_part, weights[1]),
        block_mult(real_part, weights[1]) + block_mult(imag_part, weights[0]),
    )


def block_adjoint(real_part, imag_part, weights):
    return (
        block_mult_back(real_part, weights[0]) + block_mult_back(imag_part, weights[1]),
        block_mult_back(imag_part, weights[0]) - block_mult_back(real_part, weights[1]),
    )


def latitude_tables(length):
    index_row = jnp.arange(length, dtype=jnp.int32)
    phase_angle = (
        2.0
        * math.pi
        / length
        * (index_row[:, None] * index_row[None, :] % length).astype(jnp.float32)
    )
    scaling = 1.0 / math.sqrt(length)
    return (jnp.cos(phase_angle) * scaling, -jnp.sin(phase_angle) * scaling)


def to_columns(real_part, imag_part):
    stacked = jnp.stack([real_part, imag_part])
    moved = lax.all_to_all(stacked, "space", 3, 2, tiled=True)
    return (moved[0], moved[1])


def to_rows(real_part, imag_part):
    stacked = jnp.stack([real_part, imag_part])
    moved = lax.all_to_all(stacked, "space", 2, 3, tiled=True)
    return (moved[0], moved[1])


def enter_spectrum(real_part, imag_part):
    length = real_part.shape[1] * lax.axis_size("space")
    table_cos, table_sin = latitude_tables(length)
    real_part, imag_part = to_columns(real_part, imag_part)
    return complex_latitude(table_cos, table_sin, real_part, imag_part, False)


def leave_spectrum(real_part, imag_part):
    table_cos, table_sin = latitude_tables(real_part.shape[1])
    real_part, imag_part = complex_latitude(table_cos, table_sin, real_part, imag_part, True)
    return to_rows(real_part, imag_part)


def token_sums(first_term, second_term):
    pair = jnp.stack([first_term, second_term])
    count = lax.axis_size("feat")
    bit = 1
    while bit < count:
        pair = pair + lax.ppermute(pair, "feat", [(i, i ^ bit) for i in range(count)])
        bit *= 2
    return (pair[0], pair[1])


def ring_send(block):
    count = lax.axis_size("feat")
    return [block] + [
        lax.ppermute(block, "feat", [(i, (i + shift) % count) for i in range(count)])
        for shift in range(1, count)
    ]


def ring_assemble(parts):
    count = len(parts)
    position = lax.axis_index("feat")
    block = parts[0]
    width = block.shape[-1]
    whole = jnp.zeros(block.shape[:-1] + (width * count,), block.dtype)
    for shift, moved in enumerate(parts):
        source = (position + count - shift) % count
        whole = lax.dynamic_update_slice_in_dim(whole, moved, source * width, axis=block.ndim - 1)
    return whole


def channel_share(term):
    return lax.psum_scatter(
        term.astype(jnp.bfloat16), "feat", scatter_dimension=3, tiled=True
    ).astype(jnp.float32)


def gelu_value(field):
    return 0.5 * field * (1.0 + lax.erf(field * (1.0 / math.sqrt(2.0))))


def gelu_slope(field):
    return 0.5 * (1.0 + lax.erf(field * (1.0 / math.sqrt(2.0)))) + field * jnp.exp(
        -0.5 * field * field
    ) * (1.0 / math.sqrt(2.0 * math.pi))


def spectral_forward(field, spec_w1, spec_b1, spec_w2, spec_b2, cos_fwd, sin_fwd):
    block_size = spec_w1.shape[2]
    spec_real, spec_imag = enter_spectrum(lon_forward(field, cos_fwd), lon_forward(field, sin_fwd))
    spec_shape = spec_real.shape
    bias_one = to_blocks(spec_b1, block_size)
    bias_two = to_blocks(spec_b2, block_size)
    first_real, first_imag = block_product(
        to_blocks(spec_real, block_size), to_blocks(spec_imag, block_size), spec_w1
    )
    first_real = jax.nn.relu(first_real + bias_one[0])
    first_imag = jax.nn.relu(first_imag + bias_one[1])
    second_real, second_imag = block_product(first_real, first_imag, spec_w2)
    second_real = second_real + bias_two[0]
    second_imag = second_imag + bias_two[1]
    shrunk_real = (second_real - jnp.clip(second_real, -SHRINK_LEVEL, SHRINK_LEVEL)).reshape(
        spec_shape
    )
    shrunk_imag = (second_imag - jnp.clip(second_imag, -SHRINK_LEVEL, SHRINK_LEVEL)).reshape(
        spec_shape
    )
    back = complex_latitude_inverse(shrunk_real, shrunk_imag)
    return (back, (first_real, first_imag, second_real, second_imag))


def complex_latitude_inverse(real_part, imag_part):
    table_cos, table_sin = latitude_tables(real_part.shape[1])
    return complex_latitude(table_cos, table_sin, real_part, imag_part, True)


def spectral_leave(back, cos_inv, sin_inv):
    back_real, back_imag = to_rows(*back)
    return lon_back(back_real, cos_inv) + lon_back(back_imag, sin_inv)


def spectral_backward(grad_field, saved, spec_w1, spec_w2, cos_fwd, sin_fwd, cos_inv, sin_inv):
    block_size = spec_w1.shape[2]
    first_real, first_imag, second_real, second_imag = saved
    grad_real, grad_imag = enter_spectrum(
        lon_forward(grad_field, cos_inv), lon_forward(grad_field, sin_inv)
    )
    spec_shape = grad_real.shape
    grad_real = jnp.where(
        jnp.abs(second_real) > SHRINK_LEVEL, to_blocks(grad_real, block_size), 0.0
    )
    grad_imag = jnp.where(
        jnp.abs(second_imag) > SHRINK_LEVEL, to_blocks(grad_imag, block_size), 0.0
    )
    first_grad_real, first_grad_imag = block_adjoint(grad_real, grad_imag, spec_w2)
    first_grad_real = jnp.where(first_real > 0.0, first_grad_real, 0.0)
    first_grad_imag = jnp.where(first_imag > 0.0, first_grad_imag, 0.0)
    spec_grad_real, spec_grad_imag = block_adjoint(first_grad_real, first_grad_imag, spec_w1)
    rows_real, rows_imag = leave_spectrum(
        spec_grad_real.reshape(spec_shape), spec_grad_imag.reshape(spec_shape)
    )
    return lon_back(rows_real, cos_fwd) + lon_back(rows_imag, sin_fwd)


def per_device(inputs, cotangent, spec_w1, spec_b1, spec_w2, spec_b2, up_weight, down_weight):
    full_width = up_weight.shape[0]
    block_size = spec_w1.shape[2]
    cos_fwd, sin_fwd, cos_inv, sin_inv = padded_tables(inputs.shape[2], lax.axis_size("space"))
    values = inputs.astype(jnp.float32)
    cotangent_parts = ring_send(cotangent)
    first_sum, second_sum = token_sums(jnp.sum(values, axis=-1), jnp.sum(values * values, axis=-1))
    mean_one = first_sum[..., None] / full_width
    rstd_one = lax.rsqrt(second_sum[..., None] / full_width - mean_one * mean_one + EPSILON)
    normed = (values - mean_one) * rstd_one
    block_count = spec_w1.shape[1]
    shrunk_parts, saved_parts = ([], [])
    for block in range(block_count):
        channels = slice(block * block_size, (block + 1) * block_size)
        shrunk, saved = spectral_forward(
            normed[..., channels],
            spec_w1[:, block : block + 1],
            spec_b1[:, channels],
            spec_w2[:, block : block + 1],
            spec_b2[:, channels],
            cos_fwd,
            sin_fwd,
        )
        shrunk_parts.append(shrunk)
        saved_parts.append(saved)
    shrunk_parts[-1], cotangent_parts = lax.optimization_barrier(
        (shrunk_parts[-1], cotangent_parts)
    )
    whole_cotangent = ring_assemble(cotangent_parts)
    filtered = jnp.concatenate(
        [spectral_leave(shrunk, cos_inv, sin_inv) for shrunk in shrunk_parts], axis=-1
    )
    residual = (filtered + normed + values).astype(jnp.bfloat16)
    residual_vals = residual.astype(jnp.float32)
    whole_residual = lax.all_gather(residual, "feat", axis=3, tiled=True)
    whole_vals = whole_residual.astype(jnp.float32)
    mean_two = jnp.sum(whole_vals, axis=-1, keepdims=True) / full_width
    square_two = jnp.sum(whole_vals * whole_vals, axis=-1, keepdims=True) / full_width
    rstd_two = lax.rsqrt(square_two - mean_two * mean_two + EPSILON)
    vhat = (whole_vals - mean_two) * rstd_two
    hidden = jnp.einsum(
        "brwd,dh->brwh", vhat.astype(jnp.bfloat16), up_weight, preferred_element_type=jnp.float32
    )
    activated = gelu_value(hidden).astype(jnp.bfloat16)
    mixed_term = jnp.einsum(
        "brwh,hd->brwd", activated, down_weight, preferred_element_type=jnp.float32
    )
    output = (residual_vals + channel_share(mixed_term)).astype(jnp.bfloat16)
    grad_act = jnp.einsum(
        "brwd,hd->brwh", whole_cotangent, down_weight, preferred_element_type=jnp.float32
    )
    grad_hidden = (grad_act * gelu_slope(hidden)).astype(jnp.bfloat16)
    grad_term = jnp.einsum(
        "brwh,dh->brwd", grad_hidden, up_weight, preferred_element_type=jnp.float32
    )
    total_one, total_two = token_sums(
        jnp.sum(grad_term, axis=-1), jnp.sum(grad_term * vhat, axis=-1)
    )
    grad_vhat = channel_share(grad_term)
    own_hat = (residual_vals - mean_two) * rstd_two
    grad_residual = cotangent.astype(jnp.float32) + rstd_two * (
        grad_vhat
        - total_one[..., None] / full_width
        - own_hat * (total_two[..., None] / full_width)
    )
    grad_filter = jnp.concatenate(
        [
            spectral_backward(
                grad_residual[..., block * block_size : (block + 1) * block_size],
                saved_parts[block],
                spec_w1[:, block : block + 1],
                spec_w2[:, block : block + 1],
                cos_fwd,
                sin_fwd,
                cos_inv,
                sin_inv,
            )
            for block in range(block_count)
        ],
        axis=-1,
    )
    grad_normed = grad_residual + grad_filter
    norm_one, norm_two = token_sums(
        jnp.sum(grad_normed, axis=-1), jnp.sum(grad_normed * normed, axis=-1)
    )
    grad_input = grad_residual + rstd_one * (
        grad_normed - norm_one[..., None] / full_width - normed * (norm_two[..., None] / full_width)
    )
    return (output, grad_input.astype(jnp.bfloat16))


def solution(mesh):
    return jax.shard_map(
        per_device,
        mesh=mesh,
        in_specs=(
            P(None, "space", None, "feat"),
            P(None, "space", None, "feat"),
            P(None, "feat", None, None),
            P(None, "feat"),
            P(None, "feat", None, None),
            P(None, "feat"),
            P(None, "feat"),
            P("feat", None),
        ),
        out_specs=(P(None, "space", None, "feat"), P(None, "space", None, "feat")),
        check_vma=False,
    )
```

profile of v0, /device:TPU:0, one launch (start us, length us, event | category | flops | bytes accessed | tf_op | source)
XLA Modules:
  0.0 356.5 jit_solution(820768273294857177)
XLA Ops:
  7.2 3.2 collective-permute-start.4
  17.2 17.8 %collective-permute-done = f32[2,2,3,180]{3,2,1,0:T(4,128)S(1)} collective-permute-done((f32[2,2,3,180]{3,2,1,0:T(4,128)S(1)}, f32[2,2,3,180]{3,2,1,0:T(4,128)S(1)}, u32[]{:S(2)}, u32[]{:S(2)}) %collective-permute-start) | collective-permute-done | bytes 8672 | tf_op jit(solution)/shard_map/ppermute | solution.py:127
  35.0 3.1 collective-permute-start.1
  44.0 8.3 %all-to-all-start = ((f32[2,2,3,96,128]{4,1,2,0,3:T(2,128)}), f32[2,2,3,96,128]{4,1,2,0,3:T(2,128)}, u32[]{:S(2)}, u32[]{:S(2)}) async-start(f32[2,2,3,96,128]{4,1,2,0,3:T(2,128)} %copy.147), calls=%async_computation | async-start | bytes 1179648 | tf_op jit(solution)/shard_map/all_to_all | solution.py:99
  55.2 8.9 %all-to-all-done = f32[2,2,3,96,128]{4,1,2,0,3:T(2,128)} async-done(((f32[2,2,3,96,128]{4,1,2,0,3:T(2,128)}), f32[2,2,3,96,128]{4,1,2,0,3:T(2,128)}, u32[]{:S(2)}, u32[]{:S(2)}) %all-to-all-start) | async-done | bytes 589856 | tf_op jit(solution)/shard_map/all_to_all | solution.py:99
  64.1 4.6 %all-to-all-start.2 = ((f32[2,2,3,96,128]{4,1,2,0,3:T(2,128)}), f32[2,2,3,96,128]{4,1,2,0,3:T(2,128)S(1)}, u32[]{:S(2)}, u32[]{:S(2)}) async-start(f32[2,2,3,96,128]{4,1,2,0,3:T(2,128)} %copy.161), calls=%async_computation.2 | async-start | bytes 1179648 | tf_op jit(solution)/shard_map/all_to_all | solution.py:99
  92.2 4.6 %all-to-all-start.1 = ((f32[2,2,96,3,128]{4,1,3,0,2:T(2,128)}), f32[2,2,96,3,128]{4,1,3,0,2:T(2,128)}, u32[]{:S(2)}, u32[]{:S(2)}) async-start(f32[2,2,96,3,128]{4,1,3,0,2:T(2,128)} %copy.155), calls=%async_computation.1 | async-start | bytes 1179648 | tf_op jit(solution)/shard_map/all_to_all | solution.py:105
  103.0 5.5 %all-to-all-done.1 = f32[2,2,96,3,128]{4,1,3,0,2:T(2,128)} async-done(((f32[2,2,96,3,128]{4,1,3,0,2:T(2,128)}), f32[2,2,96,3,128]{4,1,3,0,2:T(2,128)}, u32[]{:S(2)}, u32[]{:S(2)}) %all-to-all-start.1) | async-done | bytes 589856 | tf_op jit(solution)/shard_map/all_to_all | solution.py:105
  108.5 4.1 %all-to-all-start.3 = ((f32[2,2,96,3,128]{4,1,3,0,2:T(2,128)}), f32[2,2,96,3,128]{4,1,3,0,2:T(2,128)S(1)}, u32[]{:S(2)}, u32[]{:S(2)}) async-start(f32[2,2,96,3,128]{4,1,3,0,2:T(2,128)} %copy.169), calls=%async_computation.3 | async-start | bytes 1179648 | tf_op jit(solution)/shard_map/all_to_all | solution.py:105
  115.6 8.9 %all-to-all-done.3 = f32[2,2,96,3,128]{4,1,3,0,2:T(2,128)S(1)} async-done(((f32[2,2,96,3,128]{4,1,3,0,2:T(2,128)}), f32[2,2,96,3,128]{4,1,3,0,2:T(2,128)S(1)}, u32[]{:S(2)}, u32[]{:S(2)}) %all-to-all-start.3) | async-done | bytes 589856 | tf_op jit(solution)/shard_map/all_to_all | solution.py:105
  137.9 26.5 %all-gather.2.cloned.1.call-done = bf16[2,3,180,1024]{3,2,1,0:T(8,128)(2,1)} async-done(((bf16[2,3,180,256]{3,2,1,0:T(8,128)(2,1)}), bf16[2,3,180,1024]{3,2,1,0:T(8,128)(2,1)}) %all-gather.2.cloned.1.call-update) | async-done | bytes 2211856 | tf_op jit(solution)/shard_map/all_gather | solution.py:259
  167.1 5.0 %fusion.14 = f32[2,3,180,1024]{3,2,1,0:T(8,128)} fusion(bf16[2,3,180,1024]{3,2,1,0:T(8,128)(2,1)S(1)} %copy-done.32, f32[2,3,180]{2,1,0:T(4,128)S(1)} %get-tuple-element.54, f32[2,3,180]{2,1,0:T(4,128)S(1)} %get-tuple-element.53, bf16[1024,1024]{1,0:T(8,128)(2,1)S(1)} %copy-done), kind=kOutput, calls=%fused_computation.19 | convolution fusion | flops 2269347840 | bytes 8741312 | tf_op jit(solution)/shard_map/brwd,dh->brwh/dot_general | solution.py:265
  172.1 11.0 %fusion.552 = (f32[2,3,180]{2,1,0:T(4,128)S(1)}, f32[2,3,180]{2,1,0:T(4,128)S(1)}, bf16[2,3,180,1024]{3,2,1,0:T(8,128)(2,1)}) fusion(f32[2,3,180]{2,1,0:T(4,128)S(1)} %get-tuple-element.54, f32[2,3,180]{2,1,0:T(4,128)S(1)} %get-tuple-element.53, bf16[2,3,180,1024]{3,2,1,0:T(8,128)(2,1)} %all-gather.2.cloned.1.call-done, ...), kind=kOutput, calls=%fused_computation.644 | convolution fusion | flops 4548646912 | bytes 15270784 | tf_op jit(solution)/shard_map/brwh,dh->brwd/dot_general | solution.py:277
  184.7 6.2 %fusion.27 = bf16[2,3,180,1024]{3,2,1,0:T(8,128)(2,1)} fusion(bf16[1024,1024]{1,0:T(8,128)(2,1)S(1)} %copy-done.45, f32[2,3,180,1024]{3,2,1,0:T(8,128)} %fusion.14), kind=kOutput, calls=%fused_computation.35 | convolution fusion | flops 2271559680 | bytes 8732672 | tf_op jit(solution)/shard_map/brwh,hd->brwd/dot_general | solution.py:269
  200.4 15.2 %reduce-scatter.5.cloned.1.call-done = bf16[2,3,180,256]{3,2,1,0:T(8,128)(2,1)} async-done(((bf16[2,3,180,1024]{3,2,1,0:T(8,128)(2,1)}), bf16[2,3,180,256]{3,2,1,0:T(8,128)(2,1)}) %reduce-scatter.5.cloned.1.call-update) | async-done | bytes 552976 | tf_op jit(solution)/shard_map/reduce_scatter | solution.py:153
  215.6 33.3 %reduce-scatter.3.cloned.1.call-done = bf16[2,3,180,256]{3,2,1,0:T(8,128)(2,1)} async-done(((bf16[2,3,180,1024]{3,2,1,0:T(8,128)(2,1)}), bf16[2,3,180,256]{3,2,1,0:T(8,128)(2,1)}) %reduce-scatter.3.cloned.1.call-update) | async-done | bytes 552976 | tf_op jit(solution)/shard_map/reduce_scatter | solution.py:153
  253.7 7.6 %all-to-all-start.6 = ((f32[2,2,3,96,128]{4,1,2,0,3:T(2,128)}), f32[2,2,3,96,128]{4,1,2,0,3:T(2,128)S(1)}, u32[]{:S(2)}, u32[]{:S(2)}) async-start(f32[2,2,3,96,128]{4,1,2,0,3:T(2,128)} %copy.194), calls=%async_computation.8 | async-start | bytes 1179648 | tf_op jit(solution)/shard_map/all_to_all | solution.py:99
  263.7 9.5 %all-to-all-done.6 = f32[2,2,3,96,128]{4,1,2,0,3:T(2,128)S(1)} async-done(((f32[2,2,3,96,128]{4,1,2,0,3:T(2,128)}), f32[2,2,3,96,128]{4,1,2,0,3:T(2,128)S(1)}, u32[]{:S(2)}, u32[]{:S(2)}) %all-to-all-start.6) | async-done | bytes 589856 | tf_op jit(solution)/shard_map/all_to_all | solution.py:99
  273.2 4.1 %all-to-all-start.4 = ((f32[2,2,3,96,128]{4,1,2,0,3:T(2,128)}), f32[2,2,3,96,128]{4,1,2,0,3:T(2,128)S(1)}, u32[]{:S(2)}, u32[]{:S(2)}) async-start(f32[2,2,3,96,128]{4,1,2,0,3:T(2,128)} %copy.180), calls=%async_computation.6 | async-start | bytes 1179648 | tf_op jit(solution)/shard_map/all_to_all | solution.py:99
  278.6 10.6 %all-to-all-done.4 = f32[2,2,3,96,128]{4,1,2,0,3:T(2,128)S(1)} async-done(((f32[2,2,3,96,128]{4,1,2,0,3:T(2,128)}), f32[2,2,3,96,128]{4,1,2,0,3:T(2,128)S(1)}, u32[]{:S(2)}, u32[]{:S(2)}) %all-to-all-start.4) | async-done | bytes 589856 | tf_op jit(solution)/shard_map/all_to_all | solution.py:99
  299.7 4.9 %all-to-all-start.5 = ((f32[2,2,96,3,128]{4,1,3,0,2:T(2,128)}), f32[2,2,96,3,128]{4,1,3,0,2:T(2,128)}, u32[]{:S(2)}, u32[]{:S(2)}) async-start(f32[2,2,96,3,128]{4,1,3,0,2:T(2,128)} %copy.188), calls=%async_computation.7 | async-start | bytes 1179648 | tf_op jit(solution)/shard_map/all_to_all | solution.py:105
  316.4 6.9 %all-to-all-start.7 = ((f32[2,2,96,3,128]{4,1,3,0,2:T(2,128)}), f32[2,2,96,3,128]{4,1,3,0,2:T(2,128)S(1)}, u32[]{:S(2)}, u32[]{:S(2)}) async-start(f32[2,2,96,3,128]{4,1,3,0,2:T(2,128)} %copy.202), calls=%async_computation.9 | async-start | bytes 1179648 | tf_op jit(solution)/shard_map/all_to_all | solution.py:105
  325.6 9.5 %all-to-all-done.7 = f32[2,2,96,3,128]{4,1,3,0,2:T(2,128)S(1)} async-done(((f32[2,2,96,3,128]{4,1,3,0,2:T(2,128)}), f32[2,2,96,3,128]{4,1,3,0,2:T(2,128)S(1)}, u32[]{:S(2)}, u32[]{:S(2)}) %all-to-all-start.7) | async-done | bytes 589856 | tf_op jit(solution)/shard_map/all_to_all | solution.py:105
  338.8 3.5 collective-permute-done.7
  (276 shorter events, 117.6 us)
Async XLA Ops:
  7.2 159.9 %copy-start = (bf16[1024,1024]{1,0:T(8,128)(2,1)S(1)}, bf16[1024,1024]{1,0:T(8,128)(2,1)}, u32[]{:S(2)}) copy-start(bf16[1024,1024]{1,0:T(8,128)(2,1)} %param.14) | copy-start | bytes 6291460
  7.2 94.4 %collective-permute-start.4 = (bf16[2,3,180,256]{3,0,2,1:T(2,128)(2,1)}, bf16[2,3,180,256]{3,0,2,1:T(2,128)(2,1)}, u32[]{:S(2)}, u32[]{:S(2)}) collective-permute-start(bf16[2,3,180,256]{3,0,2,1:T(2,128)(2,1)} %param.9), channel_id=1, source_target_pairs={{0,3},{1,0},{2,1},{3,2},{4,7},{5,4},{6,5},{7,6},{8,11},{9,8},{10,9... | collective-permute-start | bytes 1658888 | tf_op jit(solution)/shard_map/ppermute | solution.py:135
  10.3 91.3 %collective-permute-start.3 = (bf16[2,3,180,256]{3,0,2,1:T(2,128)(2,1)}, bf16[2,3,180,256]{3,0,2,1:T(2,128)(2,1)}, u32[]{:S(2)}, u32[]{:S(2)}) collective-permute-start(bf16[2,3,180,256]{3,0,2,1:T(2,128)(2,1)} %param.9), channel_id=1, source_target_pairs={{0,2},{1,3},{2,0},{3,1},{4,6},{5,7},{6,4},{7,5},{8,10},{9,11},{10,... | collective-permute-start | bytes 1658888 | tf_op jit(solution)/shard_map/ppermute | solution.py:135
  11.0 90.7 %collective-permute-start.2 = (bf16[2,3,180,256]{3,0,2,1:T(2,128)(2,1)}, bf16[2,3,180,256]{3,0,2,1:T(2,128)(2,1)}, u32[]{:S(2)}, u32[]{:S(2)}) collective-permute-start(bf16[2,3,180,256]{3,0,2,1:T(2,128)(2,1)} %param.9), channel_id=1, source_target_pairs={{0,1},{1,2},{2,3},{3,0},{4,5},{5,6},{6,7},{7,4},{8,9},{9,10},{10,1... | collective-permute-start | bytes 1658888 | tf_op jit(solution)/shard_map/ppermute | solution.py:135
  13.5 21.4 %collective-permute-start = (f32[2,2,3,180]{3,2,1,0:T(4,128)S(1)}, f32[2,2,3,180]{3,2,1,0:T(4,128)S(1)}, u32[]{:S(2)}, u32[]{:S(2)}) collective-permute-start(f32[2,2,3,180]{3,2,1,0:T(4,128)S(1)} %pad_maximum_fusion.8), channel_id=1, source_target_pairs={{0,1},{1,0},{2,3},{3,2},{4,5},{5,4},{6,7},{7,6},{8,9},{9,8},{10,11... | collective-permute-start | bytes 25928 | tf_op jit(solution)/shard_map/ppermute | solution.py:127
  35.0 5.3 %collective-permute-start.1 = (f32[2,2,3,180]{3,2,1,0:T(4,128)S(1)}, f32[2,2,3,180]{3,2,1,0:T(4,128)S(1)}, u32[]{:S(2)}, u32[]{:S(2)}) collective-permute-start(f32[2,2,3,180]{3,2,1,0:T(4,128)S(1)} %fusion.551), channel_id=1, source_target_pairs={{0,2},{1,3},{2,0},{3,1},{4,6},{5,7},{6,4},{7,5},{8,10},{9,11},{10,... | collective-permute-start | bytes 25928 | tf_op jit(solution)/shard_map/ppermute | solution.py:127
  44.0 20.1 %all-to-all-start = ((f32[2,2,3,96,128]{4,1,2,0,3:T(2,128)}), f32[2,2,3,96,128]{4,1,2,0,3:T(2,128)}, u32[]{:S(2)}, u32[]{:S(2)}) async-start(f32[2,2,3,96,128]{4,1,2,0,3:T(2,128)} %copy.147), calls=%async_computation | async-start | bytes 1179648 | tf_op jit(solution)/shard_map/all_to_all | solution.py:99
  64.1 16.0 %all-to-all-start.2 = ((f32[2,2,3,96,128]{4,1,2,0,3:T(2,128)}), f32[2,2,3,96,128]{4,1,2,0,3:T(2,128)S(1)}, u32[]{:S(2)}, u32[]{:S(2)}) async-start(f32[2,2,3,96,128]{4,1,2,0,3:T(2,128)} %copy.161), calls=%async_computation.2 | async-start | bytes 1179648 | tf_op jit(solution)/shard_map/all_to_all | solution.py:99
  92.2 16.4 %all-to-all-start.1 = ((f32[2,2,96,3,128]{4,1,3,0,2:T(2,128)}), f32[2,2,96,3,128]{4,1,3,0,2:T(2,128)}, u32[]{:S(2)}, u32[]{:S(2)}) async-start(f32[2,2,96,3,128]{4,1,3,0,2:T(2,128)} %copy.155), calls=%async_computation.1 | async-start | bytes 1179648 | tf_op jit(solution)/shard_map/all_to_all | solution.py:105
  108.5 16.0 %all-to-all-start.3 = ((f32[2,2,96,3,128]{4,1,3,0,2:T(2,128)}), f32[2,2,96,3,128]{4,1,3,0,2:T(2,128)S(1)}, u32[]{:S(2)}, u32[]{:S(2)}) async-start(f32[2,2,96,3,128]{4,1,3,0,2:T(2,128)} %copy.169), calls=%async_computation.3 | async-start | bytes 1179648 | tf_op jit(solution)/shard_map/all_to_all | solution.py:105
  112.7 51.8 %all-gather.2.cloned.1.call-start = ((), (), s32[]{:S(2)}) async-start(), calls=%async_computation.10 | async-start | bytes 2826240 | tf_op jit(solution)/shard_map/all_gather | solution.py:259
  129.2 86.4 %reduce-scatter.5.cloned.1.call-start = ((), (), s32[]{:S(2)}) async-start(), calls=%async_computation.12 | async-start | bytes 2826240 | tf_op jit(solution)/shard_map/reduce_scatter | solution.py:153
  183.1 65.8 %reduce-scatter.3.cloned.1.call-start = ((), (), s32[]{:S(2)}) async-start(), calls=%async_computation.11 | async-start | bytes 2826240 | tf_op jit(solution)/shard_map/reduce_scatter | solution.py:153
  190.9 58.1 %copy-start.4 = (bf16[2,3,180,256]{3,2,1,0:T(8,128)(2,1)S(1)}, bf16[2,3,180,256]{3,2,1,0:T(8,128)(2,1)}, u32[]{:S(2)}) copy-start(bf16[2,3,180,256]{3,2,1,0:T(8,128)(2,1)} %fusion.102) | copy-start | bytes 1658884
  190.9 58.1 %copy-start.34 = (bf16[2,3,180,256]{3,0,2,1:T(2,128)(2,1)S(1)}, bf16[2,3,180,256]{3,0,2,1:T(2,128)(2,1)}, u32[]{:S(2)}) copy-start(bf16[2,3,180,256]{3,0,2,1:T(2,128)(2,1)} %param.9) | copy-start | bytes 1658884
  190.9 60.6 %copy-start.30 = (f32[180,91]{1,0:T(8,128)S(1)}, f32[180,91]{1,0:T(8,128)}, u32[]{:S(2)}) copy-start(f32[180,91]{1,0:T(8,128)} %copy-done.29) | copy-start | bytes 196564
  190.9 3.8 %collective-permute-start.5 = (f32[2,2,3,180]{3,2,1,0:T(4,128)S(1)}, f32[2,2,3,180]{3,2,1,0:T(4,128)S(1)}, u32[]{:S(2)}, u32[]{:S(2)}) collective-permute-start(f32[2,2,3,180]{3,2,1,0:T(4,128)S(1)} %pad_maximum_fusion.9), channel_id=1, source_target_pairs={{0,1},{1,0},{2,3},{3,2},{4,5},{5,4},{6,7},{7,6},{8,9},{9,8},{10,11... | collective-permute-start | bytes 25928 | tf_op jit(solution)/shard_map/ppermute | solution.py:127
  194.7 5.6 %collective-permute-start.6 = (f32[2,2,3,180]{3,2,1,0:T(4,128)S(1)}, f32[2,2,3,180]{3,2,1,0:T(4,128)S(1)}, u32[]{:S(2)}, u32[]{:S(2)}) collective-permute-start(f32[2,2,3,180]{3,2,1,0:T(4,128)S(1)} %fusion.550), channel_id=1, source_target_pairs={{0,2},{1,3},{2,0},{3,1},{4,6},{5,7},{6,4},{7,5},{8,10},{9,11},{10,... | collective-permute-start | bytes 25928 | tf_op jit(solution)/shard_map/ppermute | solution.py:127
  253.7 19.5 %all-to-all-start.6 = ((f32[2,2,3,96,128]{4,1,2,0,3:T(2,128)}), f32[2,2,3,96,128]{4,1,2,0,3:T(2,128)S(1)}, u32[]{:S(2)}, u32[]{:S(2)}) async-start(f32[2,2,3,96,128]{4,1,2,0,3:T(2,128)} %copy.194), calls=%async_computation.8 | async-start | bytes 1179648 | tf_op jit(solution)/shard_map/all_to_all | solution.py:99
  273.2 15.9 %all-to-all-start.4 = ((f32[2,2,3,96,128]{4,1,2,0,3:T(2,128)}), f32[2,2,3,96,128]{4,1,2,0,3:T(2,128)S(1)}, u32[]{:S(2)}, u32[]{:S(2)}) async-start(f32[2,2,3,96,128]{4,1,2,0,3:T(2,128)} %copy.180), calls=%async_computation.6 | async-start | bytes 1179648 | tf_op jit(solution)/shard_map/all_to_all | solution.py:99
  299.7 16.7 %all-to-all-start.5 = ((f32[2,2,96,3,128]{4,1,3,0,2:T(2,128)}), f32[2,2,96,3,128]{4,1,3,0,2:T(2,128)}, u32[]{:S(2)}, u32[]{:S(2)}) async-start(f32[2,2,96,3,128]{4,1,3,0,2:T(2,128)} %copy.188), calls=%async_computation.7 | async-start | bytes 1179648 | tf_op jit(solution)/shard_map/all_to_all | solution.py:105
  316.4 18.8 %all-to-all-start.7 = ((f32[2,2,96,3,128]{4,1,3,0,2:T(2,128)}), f32[2,2,96,3,128]{4,1,3,0,2:T(2,128)S(1)}, u32[]{:S(2)}, u32[]{:S(2)}) async-start(f32[2,2,96,3,128]{4,1,3,0,2:T(2,128)} %copy.202), calls=%async_computation.9 | async-start | bytes 1179648 | tf_op jit(solution)/shard_map/all_to_all | solution.py:105
  338.5 3.8 %collective-permute-start.7 = (f32[2,2,3,180]{3,2,1,0:T(4,128)S(1)}, f32[2,2,3,180]{3,2,1,0:T(4,128)S(1)}, u32[]{:S(2)}, u32[]{:S(2)}) collective-permute-start(f32[2,2,3,180]{3,2,1,0:T(4,128)S(1)} %pad_maximum_fusion.10), channel_id=1, source_target_pairs={{0,1},{1,0},{2,3},{3,2},{4,5},{5,4},{6,7},{7,6},{8,9},{9,8},{10,11... | collective-permute-start | bytes 25928 | tf_op jit(solution)/shard_map/ppermute | solution.py:127
  342.3 5.3 %collective-permute-start.8 = (f32[2,2,3,180]{3,2,1,0:T(4,128)S(1)}, f32[2,2,3,180]{3,2,1,0:T(4,128)S(1)}, u32[]{:S(2)}, u32[]{:S(2)}) collective-permute-start(f32[2,2,3,180]{3,2,1,0:T(4,128)S(1)} %fusion.549), channel_id=1, source_target_pairs={{0,2},{1,3},{2,0},{3,1},{4,6},{5,7},{6,4},{7,5},{8,10},{9,11},{10,... | collective-permute-start | bytes 25928 | tf_op jit(solution)/shard_map/ppermute | solution.py:127
  (42 other events, 226.8 us)
Sparse Core Ops, SparseCore 0:
  129.3 35.1 all-gather.1
  183.2 32.3 reduce-scatter.4
  218.2 30.7 reduce-scatter.2
where the time goes:
time: 363 us; the launch traced here: 356 us
  waiting for transfers between devices  163 us (45%)
  matrix products  68.6 us (19%)
  starting transfers between devices  61 us (17%)
  local copies, waits for them, and re-layouts  35.2 us (10%)
  between operations  15.7 us (4%)
  other arithmetic  12.5 us (3%)
    reduce_scatter x2, waiting for transfers between devices, channel_share(): lax.psum_scatter(term.astype(jnp.bfloat16), 'feat', scatter_dimension=3,...  48.5 us
    all_to_all x4, waiting for transfers between devices, to_columns(): moved = lax.all_to_all(stacked, 'space', 3, 2, tiled=True)  32 us
    ppermute x6, waiting for transfers between devices, token_sums(): lax.ppermute(pair, 'feat', [(i, i ^ bit) for i in range(count)])  31.4 us
    all_gather x1, waiting for transfers between devices, per_device(): whole_residual = lax.all_gather(residual, 'feat', axis=3, tiled=True)  26.5 us
    all_to_all x4, waiting for transfers between devices, to_rows(): moved = lax.all_to_all(stacked, 'space', 2, 3, tiled=True)  24.9 us
    all_to_all x4, starting transfers between devices, to_columns(): moved = lax.all_to_all(stacked, 'space', 3, 2, tiled=True)  24.7 us
    dot_general x32, matrix products, lat_apply(): return jnp.einsum('gh,bhkc->bgkc', table, field, precision=HIGHEST)  20.6 us
    all_to_all x4, starting transfers between devices, to_rows(): moved = lax.all_to_all(stacked, 'space', 2, 3, tiled=True)  20.6 us
  transfers between devices with their start and end apart: 20, of which 17 were waited for; matrix products, arithmetic and copies ran while one was open for 20% of the time, Pallas kernels for 0%

commit v1 on v0

--- a/solution.py
+++ b/solution.py
@@ -256,7 +256,11 @@
     )
     residual = (filtered + normed + values).astype(jnp.bfloat16)
     residual_vals = residual.astype(jnp.float32)
-    whole_residual = lax.all_gather(residual, "feat", axis=3, tiled=True)
+    size = lax.axis_size("feat")
+    repeats = [size if d == 3 else 1 for d in range(residual.ndim)]
+    whole_residual = lax.all_to_all(
+        jnp.tile(residual, repeats), "feat", split_axis=3, concat_axis=3, tiled=True
+    )
     whole_vals = whole_residual.astype(jnp.float32)
     mean_two = jnp.sum(whole_vals, axis=-1, keepdims=True) / full_width
     square_two = jnp.sum(whole_vals * whole_vals, axis=-1, keepdims=True) / full_width

time: 363 us -> 382 us (1.052)
  local copies, waits for them, and re-layouts: 35.2 us -> 51 us
    all_to_all x0 -> x1, waiting for transfers between devices: none -> 30.4 us  [per_device(): lax.all_to_all(jnp.tile(residual, repeats), 'feat', split_axis=3, concat_...]
    all_gather x1 -> x0, waiting for transfers between devices: 26.5 us -> none  [per_device(): whole_residual = lax.all_gather(residual, 'feat', axis=3, tiled=True)]
    all_to_all x0 -> x1, local copies, waits for them, and re-layouts: none -> 8.7 us  [per_device(): lax.all_to_all(jnp.tile(residual, repeats), 'feat', split_axis=3, concat_...]
    reduce_scatter x2, waiting for transfers between devices: 48.5 us -> 42.9 us  [channel_share(): lax.psum_scatter(term.astype(jnp.bfloat16), 'feat', scatter_dimension=3,...]
    all_to_all x0 -> x1, starting transfers between devices: none -> 5.37 us  [per_device(): lax.all_to_all(jnp.tile(residual, repeats), 'feat', split_axis=3, concat_...]
    another operation x0 -> x1, local copies, waits for them, and re-layouts: none -> 4.43 us  [per_device(): jnp.tile(residual, repeats)]
  transfers between devices with their start and end apart: 20 -> 20, of which waited for: 17 -> 17; matrix products, arithmetic and copies ran while one was open for 20% -> 19% of each run, Pallas kernels for 0% -> 0%
where the time goes in v1:
time: 382 us; the launch traced here: 375 us
  waiting for transfers between devices  163 us (43%)
  matrix products  68.6 us (18%)
  starting transfers between devices  64 us (17%)
  local copies, waits for them, and re-layouts  51 us (13%)
  between operations  15.9 us (4%)
  other arithmetic  11.7 us (3%)
    reduce_scatter x2, waiting for transfers between devices, channel_share(): lax.psum_scatter(term.astype(jnp.bfloat16), 'feat', scatter_dimension=3,...  42.9 us
    ppermute x6, waiting for transfers between devices, token_sums(): lax.ppermute(pair, 'feat', [(i, i ^ bit) for i in range(count)])  34 us
    all_to_all x4, waiting for transfers between devices, to_columns(): moved = lax.all_to_all(stacked, 'space', 3, 2, tiled=True)  31.3 us
    all_to_all x1, waiting for transfers between devices, per_device(): lax.all_to_all(jnp.tile(residual, repeats), 'feat', split_axis=3, concat_...  30.4 us
    all_to_all x4, waiting for transfers between devices, to_rows(): moved = lax.all_to_all(stacked, 'space', 2, 3, tiled=True)  24.9 us
    all_to_all x4, starting transfers between devices, to_columns(): moved = lax.all_to_all(stacked, 'space', 3, 2, tiled=True)  24.7 us
    dot_general x32, matrix products, lat_apply(): return jnp.einsum('gh,bhkc->bgkc', table, field, precision=HIGHEST)  20.6 us
    all_to_all x4, starting transfers between devices, to_rows(): moved = lax.all_to_all(stacked, 'space', 2, 3, tiled=True)  20.6 us
  transfers between devices with their start and end apart: 20, of which 17 were waited for; matrix products, arithmetic and copies ran while one was open for 19% of the time, Pallas kernels for 0%

profile of v1, /device:TPU:0, one launch (start us, length us, event | category | flops | bytes accessed | tf_op | source)
XLA Modules:
  0.0 374.7 jit_solution(2184129439380494470)
XLA Ops:
  17.2 17.8 %collective-permute-done = f32[2,2,3,180]{3,2,1,0:T(4,128)S(1)} collective-permute-done((f32[2,2,3,180]{3,2,1,0:T(4,128)S(1)}, f32[2,2,3,180]{3,2,1,0:T(4,128)S(1)}, u32[]{:S(2)}, u32[]{:S(2)}) %collective-permute-start) | collective-permute-done | bytes 8672 | tf_op jit(solution)/shard_map/ppermute | solution.py:127
  44.0 8.3 %all-to-all-start = ((f32[2,2,3,96,128]{4,1,2,0,3:T(2,128)}), f32[2,2,3,96,128]{4,1,2,0,3:T(2,128)}, u32[]{:S(2)}, u32[]{:S(2)}) async-start(f32[2,2,3,96,128]{4,1,2,0,3:T(2,128)} %copy.149), calls=%async_computation | async-start | bytes 1179648 | tf_op jit(solution)/shard_map/all_to_all | solution.py:99
  55.2 8.9 %all-to-all-done = f32[2,2,3,96,128]{4,1,2,0,3:T(2,128)} async-done(((f32[2,2,3,96,128]{4,1,2,0,3:T(2,128)}), f32[2,2,3,96,128]{4,1,2,0,3:T(2,128)}, u32[]{:S(2)}, u32[]{:S(2)}) %all-to-all-start) | async-done | bytes 589856 | tf_op jit(solution)/shard_map/all_to_all | solution.py:99
  64.1 4.6 %all-to-all-start.2 = ((f32[2,2,3,96,128]{4,1,2,0,3:T(2,128)}), f32[2,2,3,96,128]{4,1,2,0,3:T(2,128)S(1)}, u32[]{:S(2)}, u32[]{:S(2)}) async-start(f32[2,2,3,96,128]{4,1,2,0,3:T(2,128)} %copy.163), calls=%async_computation.2 | async-start | bytes 1179648 | tf_op jit(solution)/shard_map/all_to_all | solution.py:99
  92.2 4.6 %all-to-all-start.1 = ((f32[2,2,96,3,128]{4,1,3,0,2:T(2,128)}), f32[2,2,96,3,128]{4,1,3,0,2:T(2,128)}, u32[]{:S(2)}, u32[]{:S(2)}) async-start(f32[2,2,96,3,128]{4,1,3,0,2:T(2,128)} %copy.157), calls=%async_computation.1 | async-start | bytes 1179648 | tf_op jit(solution)/shard_map/all_to_all | solution.py:105
  103.0 5.5 %all-to-all-done.1 = f32[2,2,96,3,128]{4,1,3,0,2:T(2,128)} async-done(((f32[2,2,96,3,128]{4,1,3,0,2:T(2,128)}), f32[2,2,96,3,128]{4,1,3,0,2:T(2,128)}, u32[]{:S(2)}, u32[]{:S(2)}) %all-to-all-start.1) | async-done | bytes 589856 | tf_op jit(solution)/shard_map/all_to_all | solution.py:105
  108.5 4.1 %all-to-all-start.3 = ((f32[2,2,96,3,128]{4,1,3,0,2:T(2,128)}), f32[2,2,96,3,128]{4,1,3,0,2:T(2,128)S(1)}, u32[]{:S(2)}, u32[]{:S(2)}) async-start(f32[2,2,96,3,128]{4,1,3,0,2:T(2,128)} %copy.171), calls=%async_computation.3 | async-start | bytes 1179648 | tf_op jit(solution)/shard_map/all_to_all | solution.py:105
  115.5 8.9 %all-to-all-done.3 = f32[2,2,96,3,128]{4,1,3,0,2:T(2,128)S(1)} async-done(((f32[2,2,96,3,128]{4,1,3,0,2:T(2,128)}), f32[2,2,96,3,128]{4,1,3,0,2:T(2,128)S(1)}, u32[]{:S(2)}, u32[]{:S(2)}) %all-to-all-start.3) | async-done | bytes 589856 | tf_op jit(solution)/shard_map/all_to_all | solution.py:105
  130.2 4.4 %tile.4.clone = bf16[2,3,180,4,256]{2,0,1,4,3:T(2,128)(2,1)} broadcast(bf16[2,3,180,256]{2,0,1,3:T(2,128)(2,1)} %copy.232), dimensions={0,1,2,4} | broadcast | bytes 2764800 | tf_op jit(solution)/shard_map/tile | solution.py:262
  134.6 5.4 %all-to-all-start.4 = ((bf16[2,3,180,1024]{2,0,1,3:T(2,128)(2,1)}), bf16[2,3,180,1024]{2,0,1,3:T(2,128)(2,1)}, u32[]{:S(2)}, u32[]{:S(2)}) async-start(bf16[2,3,180,1024]{2,0,1,3:T(2,128)(2,1)} %bitcast.632), calls=%async_computation.4 | async-start | bytes 6291456 | tf_op jit(solution)/shard_map/all_to_all | solution.py:261
  148.5 30.4 %all-to-all-done.4 = bf16[2,3,180,1024]{2,0,1,3:T(2,128)(2,1)} async-done(((bf16[2,3,180,1024]{2,0,1,3:T(2,128)(2,1)}), bf16[2,3,180,1024]{2,0,1,3:T(2,128)(2,1)}, u32[]{:S(2)}, u32[]{:S(2)}) %all-to-all-start.4) | async-done | bytes 2211872 | tf_op jit(solution)/shard_map/all_to_all | solution.py:261
  178.9 8.7 %copy.178 = bf16[2,3,180,1024]{3,2,1,0:T(8,128)(2,1)} copy(bf16[2,3,180,1024]{2,0,1,3:T(2,128)(2,1)} %all-to-all-done.4) | data formatting | bytes 4423680 | tf_op jit(solution)/shard_map/all_to_all | solution.py:261
  190.1 5.0 %fusion.14 = f32[2,3,180,1024]{3,2,1,0:T(8,128)} fusion(bf16[2,3,180,1024]{3,2,1,0:T(8,128)(2,1)S(1)} %copy-done.4, f32[2,3,180]{2,1,0:T(4,128)S(1)} %get-tuple-element.54, f32[2,3,180]{2,1,0:T(4,128)S(1)} %get-tuple-element.53, bf16[1024,1024]{1,0:T(8,128)(2,1)S(1)} %copy-done), kind=kOutput, calls=%fused_computation.19 | convolution fusion | flops 2269347840 | bytes 8741312 | tf_op jit(solution)/shard_map/brwd,dh->brwh/dot_general | solution.py:269
  195.1 11.0 %fusion.552 = (f32[2,3,180]{2,1,0:T(4,128)S(1)}, f32[2,3,180]{2,1,0:T(4,128)S(1)}, bf16[2,3,180,1024]{3,2,1,0:T(8,128)(2,1)}) fusion(f32[2,3,180]{2,1,0:T(4,128)S(1)} %get-tuple-element.54, f32[2,3,180]{2,1,0:T(4,128)S(1)} %get-tuple-element.53, bf16[2,3,180,1024]{3,2,1,0:T(8,128)(2,1)} %copy.178, bf16[1024,1024]{1,0:T(8,128)(2,1)S(1)} %copy-done, ...), kind=kOutput, calls=%fused_computation.644 | convolution fusion | flops 4548646912 | bytes 15270784 | tf_op jit(solution)/shard_map/brwh,dh->brwd/dot_general | solution.py:281
  207.8 6.2 %fusion.27 = bf16[2,3,180,1024]{3,2,1,0:T(8,128)(2,1)} fusion(bf16[1024,1024]{1,0:T(8,128)(2,1)S(1)} %copy-done.47, f32[2,3,180,1024]{3,2,1,0:T(8,128)} %fusion.14), kind=kOutput, calls=%fused_computation.35 | convolution fusion | flops 2271559680 | bytes 8732672 | tf_op jit(solution)/shard_map/brwh,hd->brwd/dot_general | solution.py:273
  218.8 5.2 %collective-permute-done.6 = f32[2,2,3,180]{3,2,1,0:T(4,128)S(1)} collective-permute-done((f32[2,2,3,180]{3,2,1,0:T(4,128)S(1)}, f32[2,2,3,180]{3,2,1,0:T(4,128)S(1)}, u32[]{:S(2)}, u32[]{:S(2)}) %collective-permute-start.6) | collective-permute-done | bytes 8672 | tf_op jit(solution)/shard_map/ppermute | solution.py:127
  224.0 9.5 %reduce-scatter.5.cloned.1.call-done = bf16[2,3,180,256]{3,2,1,0:T(8,128)(2,1)} async-done(((bf16[2,3,180,1024]{3,2,1,0:T(8,128)(2,1)}), bf16[2,3,180,256]{3,2,1,0:T(8,128)(2,1)}) %reduce-scatter.5.cloned.1.call-update) | async-done | bytes 552976 | tf_op jit(solution)/shard_map/reduce_scatter | solution.py:153
  233.6 33.3 %reduce-scatter.3.cloned.1.call-done = bf16[2,3,180,256]{3,2,1,0:T(8,128)(2,1)} async-done(((bf16[2,3,180,1024]{3,2,1,0:T(8,128)(2,1)}), bf16[2,3,180,256]{3,2,1,0:T(8,128)(2,1)}) %reduce-scatter.3.cloned.1.call-update) | async-done | bytes 552976 | tf_op jit(solution)/shard_map/reduce_scatter | solution.py:153
  271.7 7.6 %all-to-all-start.7 = ((f32[2,2,3,96,128]{4,1,2,0,3:T(2,128)}), f32[2,2,3,96,128]{4,1,2,0,3:T(2,128)S(1)}, u32[]{:S(2)}, u32[]{:S(2)}) async-start(f32[2,2,3,96,128]{4,1,2,0,3:T(2,128)} %copy.198), calls=%async_computation.9 | async-start | bytes 1179648 | tf_op jit(solution)/shard_map/all_to_all | solution.py:99
  281.6 9.6 %all-to-all-done.7 = f32[2,2,3,96,128]{4,1,2,0,3:T(2,128)S(1)} async-done(((f32[2,2,3,96,128]{4,1,2,0,3:T(2,128)}), f32[2,2,3,96,128]{4,1,2,0,3:T(2,128)S(1)}, u32[]{:S(2)}, u32[]{:S(2)}) %all-to-all-start.7) | async-done | bytes 589856 | tf_op jit(solution)/shard_map/all_to_all | solution.py:99
  297.2 9.9 %all-to-all-done.5 = f32[2,2,3,96,128]{4,1,2,0,3:T(2,128)S(1)} async-done(((f32[2,2,3,96,128]{4,1,2,0,3:T(2,128)}), f32[2,2,3,96,128]{4,1,2,0,3:T(2,128)S(1)}, u32[]{:S(2)}, u32[]{:S(2)}) %all-to-all-start.5) | async-done | bytes 589856 | tf_op jit(solution)/shard_map/all_to_all | solution.py:99
  317.6 4.9 %all-to-all-start.6 = ((f32[2,2,96,3,128]{4,1,3,0,2:T(2,128)}), f32[2,2,96,3,128]{4,1,3,0,2:T(2,128)}, u32[]{:S(2)}, u32[]{:S(2)}) async-start(f32[2,2,96,3,128]{4,1,3,0,2:T(2,128)} %copy.192), calls=%async_computation.8 | async-start | bytes 1179648 | tf_op jit(solution)/shard_map/all_to_all | solution.py:105
  334.3 7.0 %all-to-all-start.8 = ((f32[2,2,96,3,128]{4,1,3,0,2:T(2,128)}), f32[2,2,96,3,128]{4,1,3,0,2:T(2,128)S(1)}, u32[]{:S(2)}, u32[]{:S(2)}) async-start(f32[2,2,96,3,128]{4,1,3,0,2:T(2,128)} %copy.206), calls=%async_computation.10 | async-start | bytes 1179648 | tf_op jit(solution)/shard_map/all_to_all | solution.py:105
  343.5 9.5 %all-to-all-done.8 = f32[2,2,96,3,128]{4,1,3,0,2:T(2,128)S(1)} async-done(((f32[2,2,96,3,128]{4,1,3,0,2:T(2,128)}), f32[2,2,96,3,128]{4,1,3,0,2:T(2,128)S(1)}, u32[]{:S(2)}, u32[]{:S(2)}) %all-to-all-start.8) | async-done | bytes 589856 | tf_op jit(solution)/shard_map/all_to_all | solution.py:105
  (282 shorter events, 128.4 us)
Async XLA Ops:
  7.2 183.0 %copy-start = (bf16[1024,1024]{1,0:T(8,128)(2,1)S(1)}, bf16[1024,1024]{1,0:T(8,128)(2,1)}, u32[]{:S(2)}) copy-start(bf16[1024,1024]{1,0:T(8,128)(2,1)} %param.14) | copy-start | bytes 6291460
  7.2 94.4 %collective-permute-start.4 = (bf16[2,3,180,256]{3,0,2,1:T(2,128)(2,1)}, bf16[2,3,180,256]{3,0,2,1:T(2,128)(2,1)}, u32[]{:S(2)}, u32[]{:S(2)}) collective-permute-start(bf16[2,3,180,256]{3,0,2,1:T(2,128)(2,1)} %param.9), channel_id=1, source_target_pairs={{0,3},{1,0},{2,1},{3,2},{4,7},{5,4},{6,5},{7,6},{8,11},{9,8},{10,9... | collective-permute-start | bytes 1658888 | tf_op jit(solution)/shard_map/ppermute | solution.py:135
  10.3 91.3 %collective-permute-start.3 = (bf16[2,3,180,256]{3,0,2,1:T(2,128)(2,1)}, bf16[2,3,180,256]{3,0,2,1:T(2,128)(2,1)}, u32[]{:S(2)}, u32[]{:S(2)}) collective-permute-start(bf16[2,3,180,256]{3,0,2,1:T(2,128)(2,1)} %param.9), channel_id=1, source_target_pairs={{0,2},{1,3},{2,0},{3,1},{4,6},{5,7},{6,4},{7,5},{8,10},{9,11},{10,... | collective-permute-start | bytes 1658888 | tf_op jit(solution)/shard_map/ppermute | solution.py:135
  11.0 90.7 %collective-permute-start.2 = (bf16[2,3,180,256]{3,0,2,1:T(2,128)(2,1)}, bf16[2,3,180,256]{3,0,2,1:T(2,128)(2,1)}, u32[]{:S(2)}, u32[]{:S(2)}) collective-permute-start(bf16[2,3,180,256]{3,0,2,1:T(2,128)(2,1)} %param.9), channel_id=1, source_target_pairs={{0,1},{1,2},{2,3},{3,0},{4,5},{5,6},{6,7},{7,4},{8,9},{9,10},{10,1... | collective-permute-start | bytes 1658888 | tf_op jit(solution)/shard_map/ppermute | solution.py:135
  13.5 21.4 %collective-permute-start = (f32[2,2,3,180]{3,2,1,0:T(4,128)S(1)}, f32[2,2,3,180]{3,2,1,0:T(4,128)S(1)}, u32[]{:S(2)}, u32[]{:S(2)}) collective-permute-start(f32[2,2,3,180]{3,2,1,0:T(4,128)S(1)} %pad_maximum_fusion.8), channel_id=1, source_target_pairs={{0,1},{1,0},{2,3},{3,2},{4,5},{5,4},{6,7},{7,6},{8,9},{9,8},{10,11... | collective-permute-start | bytes 25928 | tf_op jit(solution)/shard_map/ppermute | solution.py:127
  35.0 5.3 %collective-permute-start.1 = (f32[2,2,3,180]{3,2,1,0:T(4,128)S(1)}, f32[2,2,3,180]{3,2,1,0:T(4,128)S(1)}, u32[]{:S(2)}, u32[]{:S(2)}) collective-permute-start(f32[2,2,3,180]{3,2,1,0:T(4,128)S(1)} %fusion.551), channel_id=1, source_target_pairs={{0,2},{1,3},{2,0},{3,1},{4,6},{5,7},{6,4},{7,5},{8,10},{9,11},{10,... | collective-permute-start | bytes 25928 | tf_op jit(solution)/shard_map/ppermute | solution.py:127
  44.0 20.1 %all-to-all-start = ((f32[2,2,3,96,128]{4,1,2,0,3:T(2,128)}), f32[2,2,3,96,128]{4,1,2,0,3:T(2,128)}, u32[]{:S(2)}, u32[]{:S(2)}) async-start(f32[2,2,3,96,128]{4,1,2,0,3:T(2,128)} %copy.149), calls=%async_computation | async-start | bytes 1179648 | tf_op jit(solution)/shard_map/all_to_all | solution.py:99
  64.1 16.0 %all-to-all-start.2 = ((f32[2,2,3,96,128]{4,1,2,0,3:T(2,128)}), f32[2,2,3,96,128]{4,1,2,0,3:T(2,128)S(1)}, u32[]{:S(2)}, u32[]{:S(2)}) async-start(f32[2,2,3,96,128]{4,1,2,0,3:T(2,128)} %copy.163), calls=%async_computation.2 | async-start | bytes 1179648 | tf_op jit(solution)/shard_map/all_to_all | solution.py:99
  92.2 16.4 %all-to-all-start.1 = ((f32[2,2,96,3,128]{4,1,3,0,2:T(2,128)}), f32[2,2,96,3,128]{4,1,3,0,2:T(2,128)}, u32[]{:S(2)}, u32[]{:S(2)}) async-start(f32[2,2,96,3,128]{4,1,3,0,2:T(2,128)} %copy.157), calls=%async_computation.1 | async-start | bytes 1179648 | tf_op jit(solution)/shard_map/all_to_all | solution.py:105
  108.5 16.0 %all-to-all-start.3 = ((f32[2,2,96,3,128]{4,1,3,0,2:T(2,128)}), f32[2,2,96,3,128]{4,1,3,0,2:T(2,128)S(1)}, u32[]{:S(2)}, u32[]{:S(2)}) async-start(f32[2,2,96,3,128]{4,1,3,0,2:T(2,128)} %copy.171), calls=%async_computation.3 | async-start | bytes 1179648 | tf_op jit(solution)/shard_map/all_to_all | solution.py:105
  134.6 44.2 %all-to-all-start.4 = ((bf16[2,3,180,1024]{2,0,1,3:T(2,128)(2,1)}), bf16[2,3,180,1024]{2,0,1,3:T(2,128)(2,1)}, u32[]{:S(2)}, u32[]{:S(2)}) async-start(bf16[2,3,180,1024]{2,0,1,3:T(2,128)(2,1)} %bitcast.632), calls=%async_computation.4 | async-start | bytes 6291456 | tf_op jit(solution)/shard_map/all_to_all | solution.py:261
  140.0 93.5 %reduce-scatter.5.cloned.1.call-start = ((), (), s32[]{:S(2)}) async-start(), calls=%async_computation.12 | async-start | bytes 2826240 | tf_op jit(solution)/shard_map/reduce_scatter | solution.py:153
  206.2 60.7 %reduce-scatter.3.cloned.1.call-start = ((), (), s32[]{:S(2)}) async-start(), calls=%async_computation.11 | async-start | bytes 2826240 | tf_op jit(solution)/shard_map/reduce_scatter | solution.py:153
  213.9 53.0 %copy-start.6 = (bf16[2,3,180,256]{3,2,1,0:T(8,128)(2,1)S(1)}, bf16[2,3,180,256]{3,2,1,0:T(8,128)(2,1)}, u32[]{:S(2)}) copy-start(bf16[2,3,180,256]{3,2,1,0:T(8,128)(2,1)} %copy-done.5) | copy-start | bytes 1658884
  213.9 53.0 %copy-start.36 = (bf16[2,3,180,256]{3,0,2,1:T(2,128)(2,1)S(1)}, bf16[2,3,180,256]{3,0,2,1:T(2,128)(2,1)}, u32[]{:S(2)}) copy-start(bf16[2,3,180,256]{3,0,2,1:T(2,128)(2,1)} %param.9) | copy-start | bytes 1658884
  214.0 55.4 %copy-start.33 = (f32[180,91]{1,0:T(8,128)S(1)}, f32[180,91]{1,0:T(8,128)}, u32[]{:S(2)}) copy-start(f32[180,91]{1,0:T(8,128)} %copy-done.32) | copy-start | bytes 196564
  214.0 4.1 %collective-permute-start.5 = (f32[2,2,3,180]{3,2,1,0:T(4,128)S(1)}, f32[2,2,3,180]{3,2,1,0:T(4,128)S(1)}, u32[]{:S(2)}, u32[]{:S(2)}) collective-permute-start(f32[2,2,3,180]{3,2,1,0:T(4,128)S(1)} %pad_maximum_fusion.9), channel_id=1, source_target_pairs={{0,1},{1,0},{2,3},{3,2},{4,5},{5,4},{6,7},{7,6},{8,9},{9,8},{10,11... | collective-permute-start | bytes 25928 | tf_op jit(solution)/shard_map/ppermute | solution.py:127
  218.1 5.8 %collective-permute-start.6 = (f32[2,2,3,180]{3,2,1,0:T(4,128)S(1)}, f32[2,2,3,180]{3,2,1,0:T(4,128)S(1)}, u32[]{:S(2)}, u32[]{:S(2)}) collective-permute-start(f32[2,2,3,180]{3,2,1,0:T(4,128)S(1)} %fusion.550), channel_id=1, source_target_pairs={{0,2},{1,3},{2,0},{3,1},{4,6},{5,7},{6,4},{7,5},{8,10},{9,11},{10,... | collective-permute-start | bytes 25928 | tf_op jit(solution)/shard_map/ppermute | solution.py:127
  271.7 19.5 %all-to-all-start.7 = ((f32[2,2,3,96,128]{4,1,2,0,3:T(2,128)}), f32[2,2,3,96,128]{4,1,2,0,3:T(2,128)S(1)}, u32[]{:S(2)}, u32[]{:S(2)}) async-start(f32[2,2,3,96,128]{4,1,2,0,3:T(2,128)} %copy.198), calls=%async_computation.9 | async-start | bytes 1179648 | tf_op jit(solution)/shard_map/all_to_all | solution.py:99
  291.2 15.9 %all-to-all-start.5 = ((f32[2,2,3,96,128]{4,1,2,0,3:T(2,128)}), f32[2,2,3,96,128]{4,1,2,0,3:T(2,128)S(1)}, u32[]{:S(2)}, u32[]{:S(2)}) async-start(f32[2,2,3,96,128]{4,1,2,0,3:T(2,128)} %copy.184), calls=%async_computation.7 | async-start | bytes 1179648 | tf_op jit(solution)/shard_map/all_to_all | solution.py:99
  317.6 16.7 %all-to-all-start.6 = ((f32[2,2,96,3,128]{4,1,3,0,2:T(2,128)}), f32[2,2,96,3,128]{4,1,3,0,2:T(2,128)}, u32[]{:S(2)}, u32[]{:S(2)}) async-start(f32[2,2,96,3,128]{4,1,3,0,2:T(2,128)} %copy.192), calls=%async_computation.8 | async-start | bytes 1179648 | tf_op jit(solution)/shard_map/all_to_all | solution.py:105
  334.3 18.8 %all-to-all-start.8 = ((f32[2,2,96,3,128]{4,1,3,0,2:T(2,128)}), f32[2,2,96,3,128]{4,1,3,0,2:T(2,128)S(1)}, u32[]{:S(2)}, u32[]{:S(2)}) async-start(f32[2,2,96,3,128]{4,1,3,0,2:T(2,128)} %copy.206), calls=%async_computation.10 | async-start | bytes 1179648 | tf_op jit(solution)/shard_map/all_to_all | solution.py:105
  356.4 3.8 %collective-permute-start.7 = (f32[2,2,3,180]{3,2,1,0:T(4,128)S(1)}, f32[2,2,3,180]{3,2,1,0:T(4,128)S(1)}, u32[]{:S(2)}, u32[]{:S(2)}) collective-permute-start(f32[2,2,3,180]{3,2,1,0:T(4,128)S(1)} %pad_maximum_fusion.10), channel_id=1, source_target_pairs={{0,1},{1,0},{2,3},{3,2},{4,5},{5,4},{6,7},{7,6},{8,9},{9,8},{10,11... | collective-permute-start | bytes 25928 | tf_op jit(solution)/shard_map/ppermute | solution.py:127
  360.2 5.3 %collective-permute-start.8 = (f32[2,2,3,180]{3,2,1,0:T(4,128)S(1)}, f32[2,2,3,180]{3,2,1,0:T(4,128)S(1)}, u32[]{:S(2)}, u32[]{:S(2)}) collective-permute-start(f32[2,2,3,180]{3,2,1,0:T(4,128)S(1)} %fusion.549), channel_id=1, source_target_pairs={{0,2},{1,3},{2,0},{3,1},{4,6},{5,7},{6,4},{7,5},{8,10},{9,11},{10,... | collective-permute-start | bytes 25928 | tf_op jit(solution)/shard_map/ppermute | solution.py:127
  (44 other events, 235.7 us)
Sparse Core Ops, SparseCore 0:
  206.3 27.1 reduce-scatter.4
  236.1 30.7 reduce-scatter.2
